TPU v7x, 256 devices: a whole 4x4x8 slice. The times are simulated.
256 devices in a mesh: batch: 16 (over x_hi, z), dom: 16 (over x_lo, y, core).
Axes of the slice: x: 4 (x_hi: 2, x_lo: 2; x = x_hi * 2 + x_lo), y: 4, z: 8, core: 2. Of those that a mesh axis runs over, the one named last changes fastest.
Arguments:
- inputs: bfloat16 [32, 64, 68, 256], P('batch', 'dom'), may hold values from -70 to 70
- saved_q: bfloat16 [32, 64, 68, 256], P('batch', 'dom'), may hold values from -6.5 to 6.5
- saved_k: bfloat16 [32, 64, 68, 256], P('batch', 'dom'), may hold values from -6.5 to 6.5
- saved_v: bfloat16 [32, 64, 68, 256], P('batch', 'dom'), may hold values from -6 to 6
- attended: bfloat16 [32, 64, 68, 256], P('batch', 'dom'), may hold values from -6 to 6
- out_cot: bfloat16 [32, 64, 68, 256], P('batch', 'dom'), may hold values from -6 to 6
- conv_weight: bfloat16 [9, 256, 256], replicated, may hold values from -0.125 to 0.125
- qkv_weight: bfloat16 [256, 768], replicated, may hold values from -0.375 to 0.375
- out_weight: bfloat16 [256, 256], replicated, may hold values from -0.375 to 0.375
- norm_gain: float32 [256], replicated, may hold values from 0.5 to 1.5
- norm_shift: float32 [256], replicated, may hold values from -2.5 to 2.5
Outputs:
- input_grad: bfloat16 [32, 64, 68, 256], P('batch', 'dom')
- conv_grad: float32 [9, 256, 256], replicated
- qkv_grad: float32 [256, 768], replicated
- out_grad: float32 [256, 256], replicated
- gain_grad: float32 [256], replicated
- shift_grad: float32 [256], replicated
All inputs are finite; a program needn't handle non-finite values.
Results may differ from a plain program's by a relative error of at most 0.011.
Values may be sent and summed in bfloat16 or wider, within the bound.
No kernel may reach another device: no remote copies, remote signals or barrier semaphores. Data moves between devices by JAX's collectives and lax.ppermute only.
A program may use at most 128 MiB of HBM per device.

v0:
```python
import jax
import jax.numpy as jnp
from jax import lax
from jax.sharding import PartitionSpec as P

HEADS = 1
GROUPS = 32


EPSILON = 1e-05


def with_halo(cells, sides, width):
    for axis, dim in sides:
        count = lax.axis_size(axis)
        ends = count - 1
        head = lax.slice_in_dim(cells, 0, width, axis=dim)
        tail = lax.slice_in_dim(cells, cells.shape[dim] - width, cells.shape[dim], axis=dim)
        cells = jnp.concatenate(
            [
                lax.ppermute(tail, axis, [(i, (i + 1) % count) for i in range(ends)]),
                cells,
                lax.ppermute(head, axis, [((i + 1) % count, i) for i in range(ends)]),
            ],
            axis=dim,
        )
    return cells


def per_channel(values, group_width):
    return jnp.repeat(values, group_width, axis=-1)[:, None, None, :]


def body(
    inputs,
    saved_q,
    saved_k,
    saved_v,
    attended,
    out_cot,
    conv_weight,
    qkv_weight,
    out_weight,
    norm_gain,
    norm_shift,
):
    samples, row_count, col_count, chan_count = inputs.shape
    tok_count = row_count * col_count
    group_width = chan_count // GROUPS
    head_width = chan_count // HEADS
    score_scale = head_width ** (-0.5)
    count = row_count * col_count * group_width * lax.axis_size("dom")
    f32 = jnp.float32
    bf16 = jnp.bfloat16
    input_wide = inputs.astype(f32)
    grouped = input_wide.reshape(samples, row_count, col_count, GROUPS, group_width)
    group_sums = lax.psum((grouped.sum((1, 2, 4)), (grouped * grouped).sum((1, 2, 4))), "dom")
    group_mean = group_sums[0] / count
    group_var = group_sums[1] / count - group_mean * group_mean
    inv_std = lax.rsqrt(group_var + EPSILON)
    normed = (input_wide - per_channel(group_mean, group_width)) * per_channel(inv_std, group_width)
    pre_act = normed * norm_gain + norm_shift
    sigmoid_pre = jax.nn.sigmoid(pre_act)
    activated = (pre_act * sigmoid_pre).astype(bf16)
    padded = with_halo(activated, (("dom", 1),), 1)
    padded = jnp.pad(padded, ((0, 0), (0, 0), (1, 1), (0, 0)))

    def shifted(source, row_start, col_start):
        return source[
            :, row_start : row_start + row_count, col_start : col_start + col_count, :
        ].reshape(-1, chan_count)

    conv_sum = input_wide.reshape(-1, chan_count)
    for tap_index in range(9):
        row_off = tap_index // 3 - 1
        col_off = tap_index % 3 - 1
        conv_sum = conv_sum + jnp.dot(
            shifted(padded, 1 + row_off, 1 + col_off),
            conv_weight[tap_index],
            preferred_element_type=f32,
        )
    residual = conv_sum.astype(bf16)
    out_flat = out_cot.reshape(-1, chan_count)
    attended_flat = attended.reshape(-1, chan_count)
    out_grad = jnp.einsum("nc,nd->cd", attended_flat, out_flat, preferred_element_type=f32)
    d_attended = jnp.einsum("nd,cd->nc", out_flat, out_weight, preferred_element_type=f32).astype(
        bf16
    )

    def split_heads(values):
        return values.reshape(samples, -1, HEADS, head_width)

    def scores(left, right):
        return jnp.einsum("sqhd,skhd->shqk", left, right, preferred_element_type=f32) * score_scale

    q_rows = saved_q.reshape(samples, tok_count, chan_count)
    k_rows = saved_k.reshape(samples, tok_count, chan_count)
    v_rows = saved_v.reshape(samples, tok_count, chan_count)
    do_rows = d_attended.reshape(samples, tok_count, chan_count)
    q_heads = split_heads(q_rows)
    k_heads = split_heads(k_rows)
    v_heads = split_heads(v_rows)
    do_heads = split_heads(do_rows)
    row_dot = jnp.einsum(
        "sqhd,sqhd->sqh",
        split_heads(attended.reshape(samples, tok_count, chan_count)),
        do_heads,
        preferred_element_type=f32,
    )
    row_dot_t = row_dot.transpose(0, 2, 1)

    def grad_terms(query_heads, dout_heads, key_heads, value_heads, log_norm_t, dot_t):
        softmax_p = jnp.exp(scores(query_heads, key_heads) - log_norm_t[..., None])
        d_probs = jnp.einsum("sqhd,skhd->shqk", dout_heads, value_heads, preferred_element_type=f32)
        d_scores = (softmax_p * (d_probs - dot_t[..., None])).astype(bf16)
        return (softmax_p.astype(bf16), d_scores)

    row_max = jnp.full((samples, HEADS, tok_count), -jnp.inf, f32)
    row_total = jnp.zeros((samples, HEADS, tok_count), f32)
    logits = scores(q_heads, split_heads(lax.all_gather(k_rows, "dom", axis=1, tiled=True)))
    new_max = logits.max(-1)
    row_total = row_total * jnp.exp(row_max - new_max) + jnp.exp(logits - new_max[..., None]).sum(
        -1
    )
    row_max, row_total = (new_max, row_total)
    log_norm = row_max + jnp.log(row_total)
    shard_piece = (
        lax.all_gather(k_rows, "dom", axis=1, tiled=True),
        lax.all_gather(v_rows, "dom", axis=1, tiled=True),
    )
    key_heads = split_heads(shard_piece[0])
    value_heads = split_heads(shard_piece[1])
    p_half, d_scores = grad_terms(q_heads, do_heads, key_heads, value_heads, log_norm, row_dot_t)
    q_accum = jnp.einsum("shqk,skhd->sqhd", d_scores, key_heads, preferred_element_type=f32)
    stats_all = (
        lax.all_gather(log_norm.transpose(0, 2, 1), "dom", axis=1, tiled=True),
        lax.all_gather(row_dot, "dom", axis=1, tiled=True),
    )
    shard_piece = (
        lax.all_gather(q_rows, "dom", axis=1, tiled=True),
        lax.all_gather(do_rows, "dom", axis=1, tiled=True),
    )
    query_heads = split_heads(shard_piece[0])
    dout_heads = split_heads(shard_piece[1])
    norm_piece = stats_all[0].transpose(0, 2, 1)
    dot_piece = stats_all[1].transpose(0, 2, 1)
    p_half, d_scores = grad_terms(query_heads, dout_heads, k_heads, v_heads, norm_piece, dot_piece)
    k_accum = jnp.einsum("shqk,sqhd->skhd", d_scores, query_heads, preferred_element_type=f32)
    v_accum = jnp.einsum("shqk,sqhd->skhd", p_half, dout_heads, preferred_element_type=f32)
    k_accum, v_accum = (k_accum, v_accum)
    k_grad = (k_accum * score_scale).astype(bf16).reshape(samples, tok_count, chan_count)
    v_grad = v_accum.astype(bf16).reshape(samples, tok_count, chan_count)
    q_grad = (q_accum * score_scale).astype(bf16).reshape(samples, tok_count, chan_count)
    proj_grad = jnp.concatenate([q_grad, k_grad, v_grad], axis=-1).reshape(-1, 3 * chan_count)
    qkv_local = jnp.einsum("nc,nd->cd", residual, proj_grad, preferred_element_type=f32)
    d_residual = (
        out_flat.astype(f32)
        + jnp.einsum("nd,cd->nc", proj_grad, qkv_weight, preferred_element_type=f32)
    ).astype(bf16)
    d_res_map = d_residual.reshape(samples, row_count, col_count, chan_count)
    d_padded = with_halo(d_res_map, (("dom", 1),), 1)
    d_padded = jnp.pad(d_padded, ((0, 0), (0, 0), (1, 1), (0, 0)))
    conv_parts = []
    d_act = jnp.zeros((samples * tok_count, chan_count), f32)
    for tap_index in range(9):
        row_off = tap_index // 3 - 1
        col_off = tap_index % 3 - 1
        conv_parts.append(
            jnp.einsum(
                "nc,nd->cd",
                shifted(padded, 1 + row_off, 1 + col_off),
                d_residual,
                preferred_element_type=f32,
            )
        )
        d_act = d_act + jnp.einsum(
            "nd,cd->nc",
            shifted(d_padded, 1 - row_off, 1 - col_off),
            conv_weight[tap_index],
            preferred_element_type=f32,
        )
    conv_local = jnp.stack(conv_parts)
    d_pre = (
        d_act.reshape(samples, row_count, col_count, chan_count)
        * sigmoid_pre
        * (1.0 + pre_act * (1.0 - sigmoid_pre))
    )
    gain_local = (d_pre * normed).sum((0, 1, 2))
    shift_local = d_pre.sum((0, 1, 2))
    scaled = d_pre * norm_gain
    scaled_groups = scaled.reshape(samples, row_count, col_count, GROUPS, group_width)
    product_groups = (scaled * normed).reshape(samples, row_count, col_count, GROUPS, group_width)
    back_sums = lax.psum((scaled_groups.sum((1, 2, 4)), product_groups.sum((1, 2, 4))), "dom")
    first = back_sums[0] / count
    second = back_sums[1] / count
    input_grad = (
        d_res_map.astype(f32)
        + per_channel(inv_std, group_width)
        * (scaled - per_channel(first, group_width) - normed * per_channel(second, group_width))
    ).astype(bf16)
    out_grad, qkv_grad, conv_grad, gain_grad, shift_grad = lax.psum(
        (out_grad, qkv_local, conv_local, gain_local, shift_local), ("batch", "dom")
    )
    return (input_grad, conv_grad, qkv_grad, out_grad, gain_grad, shift_grad)


def solution(mesh):
    placed = (
        P("batch", "dom", None, None),
        P("batch", "dom", None, None),
        P("batch", "dom", None, None),
        P("batch", "dom", None, None),
        P("batch", "dom", None, None),
        P("batch", "dom", None, None),
        P(),
        P(),
        P(),
        P(),
        P(),
    )
    return jax.shard_map(
        body,
        mesh=mesh,
        in_specs=placed,
        out_specs=(P("batch", "dom", None, None), P(), P(), P(), P(), P()),
        check_vma=False,
    )
```

profile of v0, /device:TPU:120, one launch (start us, length us, event | category | flops | bytes accessed | tf_op | source)
XLA Modules:
  0.0 548.7 jit_solution(14365072272132767426)
XLA Ops:
  7.3 1.2 copy.60
  9.3 1.2 copy.59
  11.5 1.0 convolution_convert_fusion
  12.5 0.9 copy.63
  13.5 1.0 convert
  15.4 15.5 %all-gather.1 = f32[16,272,2]{1,2,0:T(2,128)S(1)} all-gather(f32[1,272,2]{1,2,0:T(2,128)S(1)} %bitcast.194), channel_id=2, replica_groups=mesh['batch'=16,'dom'=16] {'dom'}, dimensions={0}, use_global_device_ids=true | all-gather | bytes 36992 | tf_op jit(solution)/shard_map/all_gather | solution.py:137
  31.5 27.0 %all-reduce.5 = (f32[2,32]{1,0:T(2,128)S(1)}, f32[2,32]{1,0:T(2,128)S(1)}) all-reduce(f32[2,32]{1,0:T(2,128)S(1)} %reduce_sum.100, f32[2,32]{1,0:T(2,128)S(1)} %reduce_sum.81), channel_id=1, replica_groups=mesh['batch'=16,'dom'=16] {'dom'}, use_global_device_ids=true, to_apply=%region_7.8 | all-reduce | flops 128 | bytes 1024 | tf_op jit(solution)/shard_map/psum | solution.py:57
  58.5 0.9 copy_convert_fusion
  59.3 3.8 fusion.91
  63.2 1.4 exponential_reduce_fusion
  64.6 2.2 copy-done.1
  67.6 34.9 %all_gather.22 = f32[2,4352,1]{0,2,1:T(1,128)S(1)} all-gather(f32[2,272,1]{0,2,1:T(1,128)} %copy.68), channel_id=1, replica_groups=mesh['batch'=16,'dom'=16] {'dom'}, dimensions={1}, use_global_device_ids=true | all-gather | bytes 36992 | tf_op jit(solution)/shard_map/all_gather | solution.py:136
  103.2 7.5 %subtract_exponential_fusion = f32[2,4352,272]{1,2,0:T(8,128)} fusion(bf16[2,4352,256]{2,1,0:T(8,128)(2,1)} %all-gather.11.cloned.1.call-done, f32[2,4352]{1,0:T(2,128)S(1)} %copy.69, bf16[2,272,256]{2,0,1:T(2,128)(2,1)S(1)} %bitcast.185), kind=kOutput, calls=%fused_computation.1 | convolution fusion | flops 1216888832 | bytes 14239744 | tf_op jit(solution)/shard_map/sqhd,skhd->shqk/dot_general | solution.py:94
  110.7 31.2 %all-gather.13.cloned.1.call-done = bf16[2,4352,256]{2,1,0:T(8,128)(2,1)} async-done(((bf16[2,272,256]{2,1,0:T(8,128)(2,1)}), bf16[2,4352,256]{2,1,0:T(8,128)(2,1)}) %all-gather.13.cloned.1.call-update) | async-done | bytes 4456464 | tf_op jit(solution)/shard_map/all_gather | solution.py:141
  141.9 6.3 %fusion.13 = bf16[2,256,272]{1,2,0:T(8,128)(2,1)S(1)} fusion(bf16[2,4352,256]{2,1,0:T(8,128)(2,1)} %all-gather.13.cloned.1.call-done, f32[2,4352,272]{1,2,0:T(8,128)} %subtract_exponential_fusion), kind=kOutput, calls=%fused_computation.32 | convolution fusion | flops 1214660608 | bytes 14204928 | tf_op jit(solution)/shard_map/shqk,sqhd->skhd/dot_general | solution.py:149
  148.3 9.0 %fusion.12 = bf16[2,272,256]{2,1,0:T(8,128)(2,1)S(1)} fusion(bf16[2,4352,256]{2,1,0:T(8,128)(2,1)} %all-gather.11.cloned.1.call-done, f32[2,4352,272]{1,2,0:T(8,128)} %subtract_exponential_fusion, bf16[2,4352,256]{2,1,0:T(8,128)(2,1)} %all-gather.13.cloned.1.call-done, f32[2,4352]{1,0:T(2,128)S(1)} %bitcast.189, bf16[2,272,256]{2,0,1:T(2,128)(2,1)S(1)} %bitcast.187), kind=kOutput, calls=%fused_computation.31 | convolution fusion | flops 2431688704 | bytes 18974720 | tf_op jit(solution)/shard_map/shqk,sqhd->skhd/dot_general | solution.py:148
  157.3 26.3 %all-gather.9.cloned.1.call-done = bf16[2,4352,256]{2,0,1:T(2,128)(2,1)} async-done(((bf16[2,272,256]{2,0,1:T(2,128)(2,1)}), bf16[2,4352,256]{2,0,1:T(2,128)(2,1)}) %all-gather.9.cloned.1.call-update) | async-done | bytes 4456464 | tf_op jit(solution)/shard_map/all_gather | solution.py:129
  183.6 10.2 %fusion.18 = bf16[2,272,256]{2,1,0:T(8,128)(2,1)S(1)} fusion(bf16[2,4352,256]{2,1,0:T(8,128)(2,1)} %all-gather.7.cloned.1.call-done, f32[2,272,4352]{2,1,0:T(8,128)} %copy-done.1, bf16[2,272,256]{2,1,0:T(8,128)(2,1)S(1)} %bitcast.183, f32[2,272]{1,0:T(2,128)S(1)} %copy.80, f32[2,272]{1,0:T(2,128)S(1)} %log_add_fusion, ...), kind=kOutput, calls=%fused_computation.36 | convolution fusion | flops 2434056192 | bytes 18944256 | tf_op jit(solution)/shard_map/shqk,skhd->sqhd/dot_general | solution.py:134
  195.0 2.1 collective-permute-start
  197.2 3.6 collective-permute-start.1
  201.2 1.4 collective-permute-done.1
  204.2 1.0 fusion.88
  205.2 1.7 reshape.265
  207.8 1.3 fusion.57
  209.0 1.2 convolution_add_fusion.14
  211.1 1.7 reshape.269
  212.8 1.7 reshape.270
  214.6 1.7 reshape.271
  217.0 1.3 fusion.38
  218.3 1.2 convolution_add_fusion.10
  219.9 1.1 fusion.11
  221.0 1.1 reshape.273
  222.1 1.3 multiply_reduce_fusion
  223.4 6.3 %collective-permute-start.2 = (bf16[2,1,68,256]{3,2,1,0:T(8,128)(2,1)S(1)}, bf16[2,1,68,256]{3,2,1,0:T(8,128)(2,1)S(1)}, u32[]{:S(2)}, u32[]{:S(2)}) collective-permute-start(bf16[2,1,68,256]{3,2,1,0:T(8,128)(2,1)S(1)} %get-tuple-element.54), channel_id=1, source_target_pairs={{0,1},{1,2},{2,3},{3,4},{4,5},{5,6},{6,7},{7,8},{8,9},{9,10},{10,1... | collective-permute-start | bytes 208904 | tf_op jit(solution)/shard_map/ppermute | solution.py:21
  229.6 1.9 collective-permute-start.3
  231.6 2.0 convolution_bitcast_fusion
  233.6 1.9 reshape.283
  237.3 1.1 fusion.87
  239.2 2.0 fusion.30
  241.1 2.2 convolution_add_fusion.7
  243.3 1.0 reshape.276
  244.4 1.0 fusion.51
  245.4 1.7 reshape.277
  247.1 1.7 reshape.279
  248.9 1.7 reshape.281
  250.6 1.0 reshape.282
  251.7 1.0 fusion.36
  252.7 2.0 fusion.29
  254.6 2.0 fusion.28
  256.6 1.2 fusion.10
  258.1 1.0 fusion.27
  259.3 1.0 fusion.26
  260.6 1.0 fusion.25
  261.6 1.0 convolution_add_fusion.2
  262.6 1.0 fusion.24
  263.6 1.0 fusion.23
  264.6 1.0 fusion.22
  265.7 3.2 fusion.21
  269.2 26.2 %all-reduce.4 = (f32[2,32]{1,0:T(2,128)S(1)}, f32[2,32]{1,0:T(2,128)S(1)}) all-reduce(f32[2,32]{1,0:T(2,128)S(1)} %reduce_sum.106, f32[2,32]{1,0:T(2,128)S(1)} %reduce_sum.103), channel_id=1, replica_groups=mesh['batch'=16,'dom'=16] {'dom'}, use_global_device_ids=true, to_apply=%region_13.14 | all-reduce | flops 128 | bytes 1024 | tf_op jit(solution)/shard_map/psum | solution.py:193
  296.0 0.8 copy.75
  296.8 78.3 %all-reduce.2 = (f32[256]{0:T(256)}, f32[256]{0:T(256)}) all-reduce(f32[256]{0:T(256)S(1)} %get-tuple-element.24, f32[256]{0:T(256)S(1)} %get-tuple-element.27), channel_id=1, replica_groups=mesh['batch'=16,'dom'=16] {'batch','dom'}, use_global_device_ids=true, to_apply=%region_18.19 | all-reduce | flops 512 | bytes 4096 | tf_op jit(solution)/shard_map/psum | solution.py:201
  375.1 162.1 %all-reduce.8.cloned.1.call-done = (f32[9,256,256]{2,1,0:T(8,128)}, f32[256,768]{1,0:T(8,128)}, f32[256,256]{1,0:T(8,128)}) async-done(((f32[9,256,256]{2,1,0:T(8,128)}, f32[256,768]{1,0:T(8,128)}, f32[256,256]{1,0:T(8,128)}), (f32[9,256,256]{2,1,0:T(8,128)}, f32[256,768]{1,0:T(8,128)}, f32[256,256]{1,0:T(8,128)})) %all-reduce.8.cloned.1.call-update) | async-done | bytes 3407888 | tf_op jit(solution)/shard_map/psum | solution.py:201
  537.2 3.3 copy.124
  540.5 0.9 copy.125
  (125 shorter events, 15.6 us)
Async XLA Ops:
  7.2 187.4 %copy-start = (bf16[256,768]{1,0:T(8,128)(2,1)S(1)}, bf16[256,768]{1,0:T(8,128)(2,1)}, u32[]{:S(2)}) copy-start(bf16[256,768]{1,0:T(8,128)(2,1)} %param.18) | copy-start | bytes 1179652
  7.2 4.1 copy-start.19
  7.2 4.2 copy-start.23
  7.2 5.3 copy-start.18
  7.2 52.1 %all-gather.7.cloned.1.call-start = ((), (), s32[]{:S(2)}) async-start(), calls=%async_computation | async-start | bytes 4734976 | tf_op jit(solution)/shard_map/all_gather | solution.py:128
  9.3 93.9 %all-gather.11.cloned.1.call-start = ((), (), s32[]{:S(2)}) async-start(), calls=%async_computation.2 | async-start | bytes 4734976 | tf_op jit(solution)/shard_map/all_gather | solution.py:140
  10.5 4.0 copy-start.20
  11.3 130.6 %all-gather.13.cloned.1.call-start = ((), (), s32[]{:S(2)}) async-start(), calls=%async_computation.3 | async-start | bytes 4734976 | tf_op jit(solution)/shard_map/all_gather | solution.py:141
  11.4 19.6 %copy-start.2 = (bf16[2,4,68,256]{3,1,2,0:T(4,128)(2,1)S(1)}, bf16[2,4,68,256]{3,1,2,0:T(4,128)(2,1)}, u32[]{:S(2)}) copy-start(bf16[2,4,68,256]{3,1,2,0:T(4,128)(2,1)} %param.11) | copy-start | bytes 835588
  12.5 171.2 %all-gather.9.cloned.1.call-start = ((), (), s32[]{:S(2)}) async-start(), calls=%async_computation.1 | async-start | bytes 4734976 | tf_op jit(solution)/shard_map/all_gather | solution.py:129
  13.5 523.8 %all-reduce.8.cloned.1.call-start = ((), (), s32[]{:S(2)}) async-start(), calls=%async_computation.4 | async-start | bytes 6815744 | tf_op jit(solution)/shard_map/psum | solution.py:201
  63.2 3.7 copy-start.1
  110.7 37.6 %copy-start.8 = (bf16[2,4,68,256]{3,0,2,1:T(2,128)(2,1)S(1)}, bf16[2,4,68,256]{3,0,2,1:T(2,128)(2,1)}, u32[]{:S(2)}) copy-start(bf16[2,4,68,256]{3,0,2,1:T(2,128)(2,1)} %copy.63) | copy-start | bytes 835588
  148.2 45.6 %copy-start.17 = (bf16[2,256,272]{1,2,0:T(8,128)(2,1)}, bf16[2,256,272]{1,2,0:T(8,128)(2,1)S(1)}, u32[]{:S(2)}) copy-start(bf16[2,256,272]{1,2,0:T(8,128)(2,1)S(1)} %fusion.13) | copy-start | bytes 835588
  148.2 35.4 %copy-start.4 = (bf16[544,256]{1,0:T(8,128)(2,1)S(1)}, bf16[544,256]{1,0:T(8,128)(2,1)}, u32[]{:S(2)}) copy-start(bf16[544,256]{1,0:T(8,128)(2,1)} %convolution_convert_fusion) | copy-start | bytes 835588
  157.3 36.5 %copy-start.21 = (bf16[2,272,256]{2,1,0:T(8,128)(2,1)}, bf16[2,272,256]{2,1,0:T(8,128)(2,1)S(1)}, u32[]{:S(2)}) copy-start(bf16[2,272,256]{2,1,0:T(8,128)(2,1)S(1)} %fusion.12) | copy-start | bytes 835588
  193.8 0.7 copy-start.26
  195.0 6.2 %collective-permute-start = (bf16[2,1,68,256]{3,2,1,0:T(8,128)(2,1)S(1)}, bf16[2,1,68,256]{3,2,1,0:T(8,128)(2,1)S(1)}, u32[]{:S(2)}, u32[]{:S(2)}) collective-permute-start(bf16[2,1,68,256]{3,2,1,0:T(8,128)(2,1)S(1)} %get-tuple-element.58), channel_id=1, source_target_pairs={{0,1},{1,2},{2,3},{3,4},{4,5},{5,6},{6,7},{7,8},{8,9},{9,10},{10,1... | collective-permute-start | bytes 208904 | tf_op jit(solution)/shard_map/ppermute | solution.py:21
  197.2 5.4 collective-permute-start.1
  204.2 3.5 copy-start.3
  207.8 2.5 copy-start.14
  217.0 2.5 copy-start.13
  217.0 2.8 copy-start.15
  219.6 2.5 copy-start.24
  219.6 2.5 copy-start.25
  223.4 12.2 %collective-permute-start.2 = (bf16[2,1,68,256]{3,2,1,0:T(8,128)(2,1)S(1)}, bf16[2,1,68,256]{3,2,1,0:T(8,128)(2,1)S(1)}, u32[]{:S(2)}, u32[]{:S(2)}) collective-permute-start(bf16[2,1,68,256]{3,2,1,0:T(8,128)(2,1)S(1)} %get-tuple-element.54), channel_id=1, source_target_pairs={{0,1},{1,2},{2,3},{3,4},{4,5},{5,6},{6,7},{7,8},{8,9},{9,10},{10,1... | collective-permute-start | bytes 208904 | tf_op jit(solution)/shard_map/ppermute | solution.py:21
  229.6 6.0 %collective-permute-start.3 = (bf16[2,1,68,256]{3,2,1,0:T(8,128)(2,1)S(1)}, bf16[2,1,68,256]{3,2,1,0:T(8,128)(2,1)S(1)}, u32[]{:S(2)}, u32[]{:S(2)}) collective-permute-start(bf16[2,1,68,256]{3,2,1,0:T(8,128)(2,1)S(1)} %get-tuple-element.55), channel_id=1, source_target_pairs={{1,0},{2,1},{3,2},{4,3},{5,4},{6,5},{7,6},{8,7},{9,8},{10,9},{11,1... | collective-permute-start | bytes 208904 | tf_op jit(solution)/shard_map/ppermute | solution.py:23
  244.3 4.5 copy-start.7
  251.6 5.0 copy-start.10
  251.6 5.0 copy-start.11
  251.6 6.2 %copy-start.6 = (bf16[544,256]{1,0:T(8,128)(2,1)S(1)}, bf16[544,256]{1,0:T(8,128)(2,1)}, u32[]{:S(2)}) copy-start(bf16[544,256]{1,0:T(8,128)(2,1)} %reshape.277) | copy-start | bytes 835588
  257.8 2.5 copy-start.5
  260.3 3.3 copy-start.12
  268.8 27.0 %copy-start.9 = (f32[2,4,68,256]{3,2,1,0:T(8,128)S(1)}, f32[2,4,68,256]{3,2,1,0:T(8,128)}, u32[]{:S(2)}) copy-start(f32[2,4,68,256]{3,2,1,0:T(8,128)} %get-tuple-element.39) | copy-start | bytes 1671172
  537.2 3.3 copy-start.16
  537.2 4.2 copy-start.22
Sparse Core Ops, SparseCore 0:
  9.8 40.4 all-gather.6
  52.7 46.3 all-gather.10
  101.5 40.3 all-gather.12
  143.6 40.0 all-gather.8
  269.0 268.1 all-reduce.7
where the time goes:
time: 553 us; the launch traced here: 549 us
  waiting for transfers between devices  221 us (40%)
  blocking collectives  182 us (33%)
  matrix products  69.6 us (13%)
  local copies, waits for them, and re-layouts  39.9 us (7%)
  between operations  14.4 us (3%)
  starting transfers between devices  14.2 us (3%)
  other arithmetic  7.61 us (1%)
    psum x1, waiting for transfers between devices, body(): lax.psum((out_grad, qkv_local, conv_local, gain_local, shift_local), ('ba...  162 us
    psum x1, blocking collectives, body(): lax.psum((out_grad, qkv_local, conv_local, gain_local, shift_local), ('ba...  78.3 us
    all_gather x1, blocking collectives, body(): lax.all_gather(log_norm.transpose(0, 2, 1), 'dom', axis=1, tiled=True)  34.9 us
    all_gather x1, waiting for transfers between devices, body(): lax.all_gather(do_rows, 'dom', axis=1, tiled=True)  31.2 us
    psum x1, blocking collectives, body(): lax.psum((grouped.sum((1, 2, 4)), (grouped * grouped).sum((1, 2, 4))), 'd...  27 us
    all_gather x1, waiting for transfers between devices, body(): lax.all_gather(v_rows, 'dom', axis=1, tiled=True)  26.3 us
    psum x1, blocking collectives, body(): lax.psum((scaled_groups.sum((1, 2, 4)), product_groups.sum((1, 2, 4))), '...  26.2 us
    reshape x17, local copies, waits for them, and re-layouts, shifted(): return source[:, row_start:row_start + row_count, col_start:col_start + c...  18.1 us
  transfers between devices with their start and end apart: 9, of which 4 were waited for; matrix products, arithmetic and copies ran while one was open for 8% of the time, Pallas kernels for 0%

commit v1 on v0

--- a/solution.py
+++ b/solution.py
@@ -25,6 +25,61 @@
             axis=dim,
         )
     return cells
+
+
+def dom_psum(values):
+    count = lax.axis_size("dom")
+    step = 1
+    while step < count:
+        values = values + lax.ppermute(values, "dom", [(i, i ^ step) for i in range(count)])
+        step *= 2
+    return values
+
+
+def dom_gather(values):
+    count = lax.axis_size("dom")
+    me = lax.axis_index("dom")
+    values = values[None]
+    step = 1
+    while step < count:
+        got = lax.ppermute(values, "dom", [(i, i ^ step) for i in range(count)])
+        upper = (me // step) % 2 == 1
+        values = jnp.where(
+            upper, jnp.concatenate([got, values]), jnp.concatenate([values, got])
+        )
+        step *= 2
+    return values
+
+
+MESH_AXES = ("batch", "dom")
+CORE0_BITS = (1, 3, 4, 2, 7, 5, 6)
+CORE1_BITS = (4, 1, 3, 5, 2, 7, 6)
+
+
+def mesh_psum(values):
+    sizes = (lax.axis_size("batch"), lax.axis_size("dom"))
+    if sizes != (16, 16):
+        return lax.psum(values, MESH_AXES)
+    count = 256
+    me = lax.axis_index(MESH_AXES)
+    core = me % 2
+    steps = [(0, 0)] + list(zip(CORE0_BITS, CORE1_BITS))
+    chosen = []
+    for bit0, bit1 in steps:
+        half = values.shape[0] // 2
+        upper = jnp.where(core == 0, (me >> bit0) & 1, (me >> bit1) & 1) == 1
+        low, high = values[:half], values[half:]
+        send = jnp.where(upper, low, high)
+        keep = jnp.where(upper, high, low)
+        pairs = [(i, i ^ (1 << (bit0 if i % 2 == 0 else bit1))) for i in range(count)]
+        values = keep + lax.ppermute(send, MESH_AXES, pairs)
+        chosen.append((upper, pairs))
+    for upper, pairs in reversed(chosen):
+        got = lax.ppermute(values, MESH_AXES, pairs)
+        values = jnp.where(
+            upper, jnp.concatenate([got, values]), jnp.concatenate([values, got])
+        )
+    return values
 
 
 def per_channel(values, group_width):
@@ -54,7 +109,7 @@
     bf16 = jnp.bfloat16
     input_wide = inputs.astype(f32)
     grouped = input_wide.reshape(samples, row_count, col_count, GROUPS, group_width)
-    group_sums = lax.psum((grouped.sum((1, 2, 4)), (grouped * grouped).sum((1, 2, 4))), "dom")
+    group_sums = dom_psum(jnp.stack([grouped.sum((1, 2, 4)), (grouped * grouped).sum((1, 2, 4))]))
     group_mean = group_sums[0] / count
     group_var = group_sums[1] / count - group_mean * group_mean
     inv_std = lax.rsqrt(group_var + EPSILON)
@@ -132,10 +187,8 @@
     value_heads = split_heads(shard_piece[1])
     p_half, d_scores = grad_terms(q_heads, do_heads, key_heads, value_heads, log_norm, row_dot_t)
     q_accum = jnp.einsum("shqk,skhd->sqhd", d_scores, key_heads, preferred_element_type=f32)
-    stats_all = (
-        lax.all_gather(log_norm.transpose(0, 2, 1), "dom", axis=1, tiled=True),
-        lax.all_gather(row_dot, "dom", axis=1, tiled=True),
-    )
+    stats_local = dom_gather(jnp.stack([log_norm.transpose(0, 2, 1), row_dot]))
+    stats_all = stats_local.transpose(1, 2, 0, 3, 4).reshape(2, samples, -1, HEADS)
     shard_piece = (
         lax.all_gather(q_rows, "dom", axis=1, tiled=True),
         lax.all_gather(do_rows, "dom", axis=1, tiled=True),
@@ -190,7 +243,7 @@
     scaled = d_pre * norm_gain
     scaled_groups = scaled.reshape(samples, row_count, col_count, GROUPS, group_width)
     product_groups = (scaled * normed).reshape(samples, row_count, col_count, GROUPS, group_width)
-    back_sums = lax.psum((scaled_groups.sum((1, 2, 4)), product_groups.sum((1, 2, 4))), "dom")
+    back_sums = dom_psum(jnp.stack([scaled_groups.sum((1, 2, 4)), product_groups.sum((1, 2, 4))]))
     first = back_sums[0] / count
     second = back_sums[1] / count
     input_grad = (
@@ -198,9 +251,17 @@
         + per_channel(inv_std, group_width)
         * (scaled - per_channel(first, group_width) - normed * per_channel(second, group_width))
     ).astype(bf16)
-    out_grad, qkv_grad, conv_grad, gain_grad, shift_grad = lax.psum(
-        (out_grad, qkv_local, conv_local, gain_local, shift_local), ("batch", "dom")
-    )
+    parts = (out_grad, qkv_local, conv_local, gain_local, shift_local)
+    flat = jnp.concatenate([part.reshape(-1) for part in parts])
+    total = flat.shape[0]
+    padded_len = -(-total // 32768) * 32768
+    flat = mesh_psum(jnp.pad(flat, (0, padded_len - total)))
+    pieces = []
+    offset = 0
+    for part in parts:
+        pieces.append(flat[offset : offset + part.size].reshape(part.shape))
+        offset += part.size
+    out_grad, qkv_grad, conv_grad, gain_grad, shift_grad = pieces
     return (input_grad, conv_grad, qkv_grad, out_grad, gain_grad, shift_grad)
 
 

time: 553 us -> 444 us (0.80)
  blocking collectives: 182 us -> 0 us
  starting transfers between devices: 14.2 us -> 40.8 us
  waiting for transfers between devices: 221 us -> 245 us
  other arithmetic: 7.61 us -> 26 us
  local copies, waits for them, and re-layouts: 39.9 us -> 46 us
    psum x1 -> x0, waiting for transfers between devices: 162 us -> none  [body(): lax.psum((out_grad, qkv_local, conv_local, gain_local, shift_local), ('ba...]
    ppermute x0 -> x28, waiting for transfers between devices: none -> 135 us  [the longest x8 50.9 us: mesh_psum(): got = lax.ppermute(values, MESH_AXES, pairs)]
    psum x3 -> x0, blocking collectives: 131 us -> none  [the longest x1 78.3 us: body(): lax.psum((out_grad, qkv_local, conv_local, gain_local, shift_local), ('ba...]
    all_gather x2 -> x0, blocking collectives: 50.3 us -> none  [the longest x1 34.9 us: body(): lax.all_gather(log_norm.transpose(0, 2, 1), 'dom', axis=1, tiled=True)]
    ppermute x0 -> x28, starting transfers between devices: none -> 26.6 us  [the longest x8 11.4 us: mesh_psum(): values = keep + lax.ppermute(send, MESH_AXES, pairs)]
    all_gather x1, waiting for transfers between devices: 0.01 us -> 21.2 us  [body(): lax.all_gather(k_rows, 'dom', axis=1, tiled=True)]
    all_gather x1, waiting for transfers between devices: 0.02 us -> 17.1 us  [body(): lax.all_gather(q_rows, 'dom', axis=1, tiled=True)]
    select_n x0 -> x25, other arithmetic: none -> 14.9 us  [the longest x12 13 us: mesh_psum(): jnp.where(upper, jnp.concatenate([got, values]), jnp.concatenate([values,...]
  transfers between devices with their start and end apart: 9 -> 36, of which waited for: 4 -> 31; matrix products, arithmetic and copies ran while one was open for 8% -> 10% of each run, Pallas kernels for 0% -> 0%
where the time goes in v1:
time: 444 us; the launch traced here: 437 us
  waiting for transfers between devices  245 us (55%)
  matrix products  64.2 us (14%)
  local copies, waits for them, and re-layouts  46 us (10%)
  starting transfers between devices  40.8 us (9%)
  other arithmetic  26 us (6%)
  between operations  15.5 us (3%)
    ppermute x8, waiting for transfers between devices, mesh_psum(): got = lax.ppermute(values, MESH_AXES, pairs)  50.9 us
    ppermute x8, waiting for transfers between devices, mesh_psum(): values = keep + lax.ppermute(send, MESH_AXES, pairs)  48.9 us
    all_gather x1, waiting for transfers between devices, body(): lax.all_gather(do_rows, 'dom', axis=1, tiled=True)  34.9 us
    all_gather x1, waiting for transfers between devices, body(): lax.all_gather(v_rows, 'dom', axis=1, tiled=True)  34.2 us
    ppermute x8, waiting for transfers between devices, dom_psum(): lax.ppermute(values, 'dom', [(i, i ^ step) for i in range(count)])  23.9 us
    all_gather x1, waiting for transfers between devices, body(): lax.all_gather(k_rows, 'dom', axis=1, tiled=True)  21.2 us
    all_gather x1, waiting for transfers between devices, body(): lax.all_gather(q_rows, 'dom', axis=1, tiled=True)  17.1 us
    unnamed x94, local copies, waits for them, and re-layouts  14.9 us
  transfers between devices with their start and end apart: 36, of which 31 were waited for; matrix products, arithmetic and copies ran while one was open for 10% of the time, Pallas kernels for 0%

profile of v1, /device:TPU:120, one launch (start us, length us, event | category | flops | bytes accessed | tf_op | source)
XLA Modules:
  0.0 437.1 jit_solution(5991941233304587757)
XLA Ops:
  9.3 1.9 copy.46
  18.0 2.8 collective-permute-done.5
  22.0 3.9 collective-permute-done.6
  25.9 1.5 collective-permute-start.7
  27.5 2.0 collective-permute-done.7
  29.5 21.2 %all-gather.5.cloned.1.call-done = bf16[2,4352,256]{2,1,0:T(8,128)(2,1)} async-done(((bf16[2,272,256]{2,1,0:T(8,128)(2,1)}), bf16[2,4352,256]{2,1,0:T(8,128)(2,1)}) %all-gather.5.cloned.1.call-update) | async-done | bytes 4456464 | tf_op jit(solution)/shard_map/all_gather | solution.py:183
  50.7 3.8 fusion.106
  56.0 2.2 copy-done.2
  58.8 34.2 %all-gather.7.cloned.1.call-done = bf16[2,4352,256]{2,0,1:T(2,128)(2,1)} async-done(((bf16[2,272,256]{2,0,1:T(2,128)(2,1)}), bf16[2,4352,256]{2,0,1:T(2,128)(2,1)}) %all-gather.7.cloned.1.call-update) | async-done | bytes 4456464 | tf_op jit(solution)/shard_map/all_gather | solution.py:184
  93.0 10.2 %fusion.19 = bf16[2,272,256]{2,1,0:T(8,128)(2,1)S(1)} fusion(bf16[2,4352,256]{2,1,0:T(8,128)(2,1)} %all-gather.5.cloned.1.call-done, f32[2,272,4352]{2,1,0:T(8,128)} %copy-done.2, bf16[2,272,256]{2,1,0:T(8,128)(2,1)S(1)} %bitcast.216, f32[2,272]{1,0:T(2,128)S(1)} %copy.64, f32[2,272]{1,0:T(2,128)S(1)} %log_add_fusion, ...), kind=kOutput, calls=%fused_computation.44 | convolution fusion | flops 2434056192 | bytes 18944256 | tf_op jit(solution)/shard_map/shqk,skhd->sqhd/dot_general | solution.py:189
  104.4 2.7 collective-permute-done.1
  107.1 2.2 collective-permute-start.2
  109.3 3.9 collective-permute-done.2
  114.0 4.5 %collective-permute-done.3 = f32[8,2,2,272,1]{3,0,2,4,1:T(8,128)S(1)} collective-permute-done((f32[8,2,2,272,1]{3,0,2,4,1:T(8,128)S(1)}, f32[8,2,2,272,1]{3,0,2,4,1:T(8,128)S(1)}, u32[]{:S(2)}, u32[]{:S(2)}) %collective-permute-start.3) | collective-permute-done | bytes 34848 | tf_op jit(solution)/shard_map/ppermute | solution.py:45
  118.8 17.1 %all-gather.9.cloned.1.call-done = bf16[2,4352,256]{2,1,0:T(8,128)(2,1)} async-done(((bf16[2,272,256]{2,1,0:T(8,128)(2,1)}), bf16[2,4352,256]{2,1,0:T(8,128)(2,1)}) %all-gather.9.cloned.1.call-update) | async-done | bytes 4456464 | tf_op jit(solution)/shard_map/all_gather | solution.py:193
  135.9 7.5 %subtract_exponential_fusion = f32[2,4352,272]{1,2,0:T(8,128)} fusion(bf16[2,4352,256]{2,1,0:T(8,128)(2,1)} %all-gather.9.cloned.1.call-done, f32[2,4352]{1,0:T(2,128)S(1)} %sub.118, bf16[2,272,256]{2,0,1:T(2,128)(2,1)S(1)} %bitcast.218), kind=kOutput, calls=%fused_computation.1 | convolution fusion | flops 1216888832 | bytes 14239744 | tf_op jit(solution)/shard_map/sqhd,skhd->shqk/dot_general | solution.py:149
  143.3 34.9 %all-gather.11.cloned.1.call-done = bf16[2,4352,256]{2,1,0:T(8,128)(2,1)} async-done(((bf16[2,272,256]{2,1,0:T(8,128)(2,1)}), bf16[2,4352,256]{2,1,0:T(8,128)(2,1)}) %all-gather.11.cloned.1.call-update) | async-done | bytes 4456464 | tf_op jit(solution)/shard_map/all_gather | solution.py:194
  178.2 6.3 %fusion.14 = bf16[2,256,272]{1,2,0:T(8,128)(2,1)S(1)} fusion(bf16[2,4352,256]{2,1,0:T(8,128)(2,1)} %all-gather.11.cloned.1.call-done, f32[2,4352,272]{1,2,0:T(8,128)} %subtract_exponential_fusion), kind=kOutput, calls=%fused_computation.40 | convolution fusion | flops 1214660608 | bytes 14204928 | tf_op jit(solution)/shard_map/shqk,sqhd->skhd/dot_general | solution.py:202
  184.6 9.0 %fusion.13 = bf16[2,272,256]{2,1,0:T(8,128)(2,1)S(1)} fusion(bf16[2,4352,256]{2,1,0:T(8,128)(2,1)} %all-gather.9.cloned.1.call-done, f32[2,4352,272]{1,2,0:T(8,128)} %subtract_exponential_fusion, bf16[2,4352,256]{2,1,0:T(8,128)(2,1)} %all-gather.11.cloned.1.call-done, f32[2,4352]{1,0:T(2,128)S(1)} %sub.121, bf16[2,272,256]{2,0,1:T(2,128)(2,1)S(1)} %bitcast.220), kind=kOutput, calls=%fused_computation.39 | convolution fusion | flops 2431688704 | bytes 18974720 | tf_op jit(solution)/shard_map/shqk,sqhd->skhd/dot_general | solution.py:201
  194.1 2.1 collective-permute-start.8
  196.2 3.6 collective-permute-start.9
  204.4 1.7 reshape.731
  206.1 1.7 reshape.730
  217.5 1.9 multiply_reduce_fusion
  219.4 6.3 %collective-permute-start.14 = (bf16[2,1,68,256]{3,2,1,0:T(8,128)(2,1)S(1)}, bf16[2,1,68,256]{3,2,1,0:T(8,128)(2,1)S(1)}, u32[]{:S(2)}, u32[]{:S(2)}) collective-permute-start(bf16[2,1,68,256]{3,2,1,0:T(8,128)(2,1)S(1)} %get-tuple-element.41), channel_id=1, source_target_pairs={{0,1},{1,2},{2,3},{3,4},{4,5},{5,6},{6,7},{7,8},{8,9},{9,10},{10,1... | collective-permute-start | bytes 208904 | tf_op jit(solution)/shard_map/ppermute | solution.py:21
  225.7 1.9 collective-permute-start.15
  236.9 2.1 convolution_add_fusion.7
  244.5 3.0 fusion.22
  248.8 2.0 fusion.30
  257.9 3.0 copy.67
  261.9 1.5 fusion.6
  264.3 3.9 collective-permute-start.16
  268.1 3.7 collective-permute-done.16
  271.8 2.2 select_add_fusion
  275.4 13.0 %collective-permute-done.17 = f32[221184]{0:T(1024)S(1)} collective-permute-done((f32[221184]{0:T(1024)S(1)}, f32[221184]{0:T(1024)S(1)}, u32[]{:S(2)}, u32[]{:S(2)}) %collective-permute-start.17) | collective-permute-done | bytes 884768 | tf_op jit(solution)/shard_map/ppermute | solution.py:75
  288.5 1.6 select_add_fusion.1
  290.2 8.3 %collective-permute-done.18 = f32[110592]{0:T(1024)S(1)} collective-permute-done((f32[110592]{0:T(1024)S(1)}, f32[110592]{0:T(1024)S(1)}, u32[]{:S(2)}, u32[]{:S(2)}) %collective-permute-start.18) | collective-permute-done | bytes 442400 | tf_op jit(solution)/shard_map/ppermute | solution.py:75
  299.4 5.4 %collective-permute-done.19 = f32[55296]{0:T(1024)S(1)} collective-permute-done((f32[55296]{0:T(1024)S(1)}, f32[55296]{0:T(1024)S(1)}, u32[]{:S(2)}, u32[]{:S(2)}) %collective-permute-start.19) | collective-permute-done | bytes 221216 | tf_op jit(solution)/shard_map/ppermute | solution.py:75
  305.0 6.2 %collective-permute-done.20 = f32[27648]{0:T(1024)S(1)} collective-permute-done((f32[27648]{0:T(1024)S(1)}, f32[27648]{0:T(1024)S(1)}, u32[]{:S(2)}, u32[]{:S(2)}) %collective-permute-start.20) | collective-permute-done | bytes 110624 | tf_op jit(solution)/shard_map/ppermute | solution.py:75
  311.3 2.8 collective-permute-start.21
  314.1 3.0 collective-permute-done.21
  317.9 4.4 %collective-permute-done.22 = f32[6912]{0:T(1024)S(1)} collective-permute-done((f32[6912]{0:T(1024)S(1)}, f32[6912]{0:T(1024)S(1)}, u32[]{:S(2)}, u32[]{:S(2)}) %collective-permute-start.22) | collective-permute-done | bytes 27680 | tf_op jit(solution)/shard_map/ppermute | solution.py:75
  322.3 2.8 collective-permute-start.23
  325.1 4.9 %collective-permute-done.23 = f32[3456]{0:T(1024)S(1)} collective-permute-done((f32[3456]{0:T(1024)S(1)}, f32[3456]{0:T(1024)S(1)}, u32[]{:S(2)}, u32[]{:S(2)}) %collective-permute-start.23) | collective-permute-done | bytes 13856 | tf_op jit(solution)/shard_map/ppermute | solution.py:75
  330.0 2.7 collective-permute-start.24
  332.8 4.9 %collective-permute-done.24 = f32[3456]{0:T(1024)S(1)} collective-permute-done((f32[3456]{0:T(1024)S(1)}, f32[3456]{0:T(1024)S(1)}, u32[]{:S(2)}, u32[]{:S(2)}) %collective-permute-start.24) | collective-permute-done | bytes 13856 | tf_op jit(solution)/shard_map/ppermute | solution.py:78
  338.2 6.0 %collective-permute-done.25 = f32[6912]{0:T(1024)S(1)} collective-permute-done((f32[6912]{0:T(1024)S(1)}, f32[6912]{0:T(1024)S(1)}, u32[]{:S(2)}, u32[]{:S(2)}) %collective-permute-start.25) | collective-permute-done | bytes 27680 | tf_op jit(solution)/shard_map/ppermute | solution.py:78
  344.1 2.8 collective-permute-start.26
  347.0 3.6 collective-permute-done.26
  350.6 7.4 %collective-permute-done.27 = f32[27648]{0:T(1024)S(1)} collective-permute-done((f32[27648]{0:T(1024)S(1)}, f32[27648]{0:T(1024)S(1)}, u32[]{:S(2)}, u32[]{:S(2)}) %collective-permute-start.27) | collective-permute-done | bytes 110624 | tf_op jit(solution)/shard_map/ppermute | solution.py:78
  358.2 8.3 %collective-permute-done.28 = f32[55296]{0:T(1024)S(1)} collective-permute-done((f32[55296]{0:T(1024)S(1)}, f32[55296]{0:T(1024)S(1)}, u32[]{:S(2)}, u32[]{:S(2)}) %collective-permute-start.28) | collective-permute-done | bytes 221216 | tf_op jit(solution)/shard_map/ppermute | solution.py:78
  367.2 7.8 %collective-permute-done.29 = f32[110592]{0:T(1024)S(1)} collective-permute-done((f32[110592]{0:T(1024)S(1)}, f32[110592]{0:T(1024)S(1)}, u32[]{:S(2)}, u32[]{:S(2)}) %collective-permute-start.29) | collective-permute-done | bytes 442400 | tf_op jit(solution)/shard_map/ppermute | solution.py:78
  375.7 13.0 %collective-permute-done.30 = f32[221184]{0:T(1024)S(1)} collective-permute-done((f32[221184]{0:T(1024)S(1)}, f32[221184]{0:T(1024)S(1)}, u32[]{:S(2)}, u32[]{:S(2)}) %collective-permute-start.30) | collective-permute-done | bytes 884768 | tf_op jit(solution)/shard_map/ppermute | solution.py:78
  391.1 2.9 collective-permute-done.10
  394.1 3.6 collective-permute-done.11
  397.7 5.1 %collective-permute-done.12 = f32[2,2,32]{2,1,0:T(2,128)S(1)} collective-permute-done((f32[2,2,32]{2,1,0:T(2,128)S(1)}, f32[2,2,32]{2,1,0:T(2,128)S(1)}, u32[]{:S(2)}, u32[]{:S(2)}) %collective-permute-start.12) | collective-permute-done | bytes 544 | tf_op jit(solution)/shard_map/ppermute | solution.py:34
  403.0 3.6 collective-permute-done.13
  410.9 1.9 concatenate.347
  412.9 2.5 maximum_select_fusion.4
  416.5 3.5 maximum_select_fusion.2
  419.9 3.0 maximum_select_fusion
  423.8 1.8 reshape.748
  426.5 1.8 concatenate.345
  428.4 1.7 fusion.37
  (266 shorter events, 68.8 us)
Async XLA Ops:
  7.2 186.4 %copy-start = (bf16[256,768]{1,0:T(8,128)(2,1)S(1)}, bf16[256,768]{1,0:T(8,128)(2,1)}, u32[]{:S(2)}) copy-start(bf16[256,768]{1,0:T(8,128)(2,1)} %param.18) | copy-start | bytes 1179652
  7.2 4.2 copy-start.30
  7.2 5.2 %copy-start.31 = (bf16[2,4,68,256]{3,1,2,0:T(4,128)(2,1)S(1)}, bf16[2,4,68,256]{3,1,2,0:T(4,128)(2,1)}, u32[]{:S(2)}) copy-start(bf16[2,4,68,256]{3,1,2,0:T(4,128)(2,1)} %param.16) | copy-start | bytes 835588
  7.2 5.3 %copy-start.35 = (bf16[256,256]{1,0:T(8,128)(2,1)S(1)}, bf16[256,256]{1,0:T(8,128)(2,1)}, u32[]{:S(2)}) copy-start(bf16[256,256]{1,0:T(8,128)(2,1)} %param.19) | copy-start | bytes 393220
  7.2 43.5 %all-gather.5.cloned.1.call-start = ((), (), s32[]{:S(2)}) async-start(), calls=%async_computation | async-start | bytes 4734976 | tf_op jit(solution)/shard_map/all_gather | solution.py:183
  9.2 4.3 copy-start.7
  9.3 83.7 %all-gather.7.cloned.1.call-start = ((), (), s32[]{:S(2)}) async-start(), calls=%async_computation.1 | async-start | bytes 4734976 | tf_op jit(solution)/shard_map/all_gather | solution.py:184
  11.3 3.9 copy-start.32
  11.3 124.6 %all-gather.9.cloned.1.call-start = ((), (), s32[]{:S(2)}) async-start(), calls=%async_computation.2 | async-start | bytes 4734976 | tf_op jit(solution)/shard_map/all_gather | solution.py:193
  12.3 165.9 %all-gather.11.cloned.1.call-start = ((), (), s32[]{:S(2)}) async-start(), calls=%async_computation.3 | async-start | bytes 4734976 | tf_op jit(solution)/shard_map/all_gather | solution.py:194
  14.0 3.1 collective-permute-start.4
  15.8 38.7 %copy-start.10 = (f32[32,2,8,128]{3,1,2,0:T(2,128)}, f32[32,2,8,128]{3,1,2,0:T(2,128)S(1)}, u32[]{:S(2)}) copy-start(f32[32,2,8,128]{3,1,2,0:T(2,128)S(1)} %copy.66) | copy-start | bytes 786436
  17.1 3.7 collective-permute-start.5
  20.8 5.1 %collective-permute-start.6 = (f32[2,2,32]{2,1,0:T(2,128)S(1)}, f32[2,2,32]{2,1,0:T(2,128)S(1)}, u32[]{:S(2)}, u32[]{:S(2)}) collective-permute-start(f32[2,2,32]{2,1,0:T(2,128)S(1)} %fusion.154), channel_id=1, source_target_pairs={{0,4},{1,5},{2,6},{3,7},{4,0},{5,1},{6,2},{7,3},{8,12},{9,13},{10,... | collective-permute-start | bytes 1544 | tf_op jit(solution)/shard_map/ppermute | solution.py:34
  25.9 3.6 collective-permute-start.7
  54.5 3.7 copy-start.2
  54.6 38.4 %copy-start.12 = (bf16[544,256]{1,0:T(8,128)(2,1)S(1)}, bf16[544,256]{1,0:T(8,128)(2,1)}, u32[]{:S(2)}) copy-start(bf16[544,256]{1,0:T(8,128)(2,1)} %convolution_convert_fusion) | copy-start | bytes 835588
  58.3 45.0 %collective-permute-start = (f32[1,2,2,272,1]{3,4,2,1,0:T(1,128)S(1)}, f32[1,2,2,272,1]{3,4,2,1,0:T(1,128)S(1)}, u32[]{:S(2)}, u32[]{:S(2)}) collective-permute-start(f32[1,2,2,272,1]{3,4,2,1,0:T(1,128)S(1)} %get-tuple-element.50), channel_id=1, source_target_pairs={{0,1},{1,0},{2,3},{3,2},{4,5},{5,4},{6,7},{7,6},{8,9},{9,8},{10,11... | collective-permute-start | bytes 13064 | tf_op jit(solution)/shard_map/ppermute | solution.py:45
  103.2 90.4 %copy-start.40 = (bf16[2,272,256]{2,1,0:T(8,128)(2,1)}, bf16[2,272,256]{2,1,0:T(8,128)(2,1)S(1)}, u32[]{:S(2)}) copy-start(bf16[2,272,256]{2,1,0:T(8,128)(2,1)S(1)} %fusion.19) | copy-start | bytes 835588
  103.3 3.8 collective-permute-start.1
  107.1 6.1 %collective-permute-start.2 = (f32[4,2,2,272,1]{3,0,2,1,4:T(4,128)S(1)}, f32[4,2,2,272,1]{3,0,2,1,4:T(4,128)S(1)}, u32[]{:S(2)}, u32[]{:S(2)}) collective-permute-start(f32[4,2,2,272,1]{3,0,2,1,4:T(4,128)S(1)} %maximum_select_fusion.14), channel_id=1, source_target_pairs={{0,4},{1,5},{2,6},{3,7},{4,0},{5,1},{6,2},{7,3},{8,12},{9,13},{10,... | collective-permute-start | bytes 52232 | tf_op jit(solution)/shard_map/ppermute | solution.py:45
  113.2 5.3 %collective-permute-start.3 = (f32[8,2,2,272,1]{3,0,2,4,1:T(8,128)S(1)}, f32[8,2,2,272,1]{3,0,2,4,1:T(8,128)S(1)}, u32[]{:S(2)}, u32[]{:S(2)}) collective-permute-start(f32[8,2,2,272,1]{3,0,2,4,1:T(8,128)S(1)} %fusion.81), channel_id=1, source_target_pairs={{0,8},{1,9},{2,10},{3,11},{4,12},{5,13},{6,14},{7,15},{8,0},{9,1},... | collective-permute-start | bytes 104456 | tf_op jit(solution)/shard_map/ppermute | solution.py:45
  143.3 41.2 %copy-start.19 = (bf16[2,4,68,256]{3,0,2,1:T(2,128)(2,1)S(1)}, bf16[2,4,68,256]{3,0,2,1:T(2,128)(2,1)}, u32[]{:S(2)}) copy-start(bf16[2,4,68,256]{3,0,2,1:T(2,128)(2,1)} %copy.46) | copy-start | bytes 835588
  184.6 9.0 %copy-start.28 = (bf16[2,256,272]{1,2,0:T(8,128)(2,1)}, bf16[2,256,272]{1,2,0:T(8,128)(2,1)S(1)}, u32[]{:S(2)}) copy-start(bf16[2,256,272]{1,2,0:T(8,128)(2,1)S(1)} %fusion.14) | copy-start | bytes 835588
  193.6 8.1 %copy-start.33 = (bf16[2,272,256]{2,1,0:T(8,128)(2,1)}, bf16[2,272,256]{2,1,0:T(8,128)(2,1)S(1)}, u32[]{:S(2)}) copy-start(bf16[2,272,256]{2,1,0:T(8,128)(2,1)S(1)} %fusion.13) | copy-start | bytes 835588
  194.1 6.1 %collective-permute-start.8 = (bf16[2,1,68,256]{3,2,1,0:T(8,128)(2,1)S(1)}, bf16[2,1,68,256]{3,2,1,0:T(8,128)(2,1)S(1)}, u32[]{:S(2)}, u32[]{:S(2)}) collective-permute-start(bf16[2,1,68,256]{3,2,1,0:T(8,128)(2,1)S(1)} %get-tuple-element.45), channel_id=1, source_target_pairs={{0,1},{1,2},{2,3},{3,4},{4,5},{5,6},{6,7},{7,8},{8,9},{9,10},{10,1... | collective-permute-start | bytes 208904 | tf_op jit(solution)/shard_map/ppermute | solution.py:21
  196.2 5.4 %collective-permute-start.9 = (bf16[2,1,68,256]{3,2,1,0:T(8,128)(2,1)S(1)}, bf16[2,1,68,256]{3,2,1,0:T(8,128)(2,1)S(1)}, u32[]{:S(2)}, u32[]{:S(2)}) collective-permute-start(bf16[2,1,68,256]{3,2,1,0:T(8,128)(2,1)S(1)} %get-tuple-element.46), channel_id=1, source_target_pairs={{1,0},{2,1},{3,2},{4,3},{5,4},{6,5},{7,6},{8,7},{9,8},{10,9},{11,1... | collective-permute-start | bytes 208904 | tf_op jit(solution)/shard_map/ppermute | solution.py:23
  203.4 6.0 %copy-start.9 = (bf16[9,256,256]{2,1,0:T(8,128)(2,1)S(1)}, bf16[9,256,256]{2,1,0:T(8,128)(2,1)}, u32[]{:S(2)}) copy-start(bf16[9,256,256]{2,1,0:T(8,128)(2,1)} %param.17) | copy-start | bytes 3538948
  208.7 3.5 copy-start.25
  219.4 9.2 %collective-permute-start.14 = (bf16[2,1,68,256]{3,2,1,0:T(8,128)(2,1)S(1)}, bf16[2,1,68,256]{3,2,1,0:T(8,128)(2,1)S(1)}, u32[]{:S(2)}, u32[]{:S(2)}) collective-permute-start(bf16[2,1,68,256]{3,2,1,0:T(8,128)(2,1)S(1)} %get-tuple-element.41), channel_id=1, source_target_pairs={{0,1},{1,2},{2,3},{3,4},{4,5},{5,6},{6,7},{7,8},{8,9},{9,10},{10,1... | collective-permute-start | bytes 208904 | tf_op jit(solution)/shard_map/ppermute | solution.py:21
  225.7 3.9 collective-permute-start.15
  233.6 9.1 %copy-start.15 = (bf16[544,256]{1,0:T(8,128)(2,1)}, bf16[544,256]{1,0:T(8,128)(2,1)S(1)}, u32[]{:S(2)}) copy-start(bf16[544,256]{1,0:T(8,128)(2,1)S(1)} %reshape.740) | copy-start | bytes 835588
  234.7 6.6 %copy-start.17 = (bf16[544,256]{1,0:T(8,128)(2,1)}, bf16[544,256]{1,0:T(8,128)(2,1)S(1)}, u32[]{:S(2)}) copy-start(bf16[544,256]{1,0:T(8,128)(2,1)S(1)} %reshape.739) | copy-start | bytes 835588
  240.0 3.0 copy-start.13
  247.5 3.3 copy-start.18
  247.5 4.3 copy-start.16
  248.8 7.1 %copy-start.22 = (bf16[544,256]{1,0:T(8,128)(2,1)S(1)}, bf16[544,256]{1,0:T(8,128)(2,1)}, u32[]{:S(2)}) copy-start(bf16[544,256]{1,0:T(8,128)(2,1)} %reshape.744) | copy-start | bytes 835588
  250.8 6.1 %copy-start.14 = (bf16[544,256]{1,0:T(8,128)(2,1)S(1)}, bf16[544,256]{1,0:T(8,128)(2,1)}, u32[]{:S(2)}) copy-start(bf16[544,256]{1,0:T(8,128)(2,1)} %copy-done.13) | copy-start | bytes 835588
  257.9 3.0 copy-start.4
  264.3 7.6 %collective-permute-start.16 = (f32[442368]{0:T(1024)}, f32[442368]{0:T(1024)}, u32[]{:S(2)}, u32[]{:S(2)}) collective-permute-start(f32[442368]{0:T(1024)} %fusion.6), channel_id=1, source_target_pairs={{0,1},{1,0},{2,3},{3,2},{4,5},{5,4},{6,7},{7,6},{8,9},{9,8},{10,11... | collective-permute-start | bytes 5308424 | tf_op jit(solution)/shard_map/ppermute | solution.py:75
  275.3 13.1 %collective-permute-start.17 = (f32[221184]{0:T(1024)S(1)}, f32[221184]{0:T(1024)S(1)}, u32[]{:S(2)}, u32[]{:S(2)}) collective-permute-start(f32[221184]{0:T(1024)S(1)} %slice_select_fusion), channel_id=1, source_target_pairs={{0,2},{1,17},{2,0},{3,19},{4,6},{5,21},{6,4},{7,23},{8,10},{9,25},... | collective-permute-start | bytes 2654216 | tf_op jit(solution)/shard_map/ppermute | solution.py:75
  290.1 8.4 %collective-permute-start.18 = (f32[110592]{0:T(1024)S(1)}, f32[110592]{0:T(1024)S(1)}, u32[]{:S(2)}, u32[]{:S(2)}) collective-permute-start(f32[110592]{0:T(1024)S(1)} %slice_select_fusion.1), channel_id=1, source_target_pairs={{0,8},{1,3},{2,10},{3,1},{4,12},{5,7},{6,14},{7,5},{8,0},{9,11},{1... | collective-permute-start | bytes 1327112 | tf_op jit(solution)/shard_map/ppermute | solution.py:75
  298.6 6.3 %collective-permute-start.19 = (f32[55296]{0:T(1024)S(1)}, f32[55296]{0:T(1024)S(1)}, u32[]{:S(2)}, u32[]{:S(2)}) collective-permute-start(f32[55296]{0:T(1024)S(1)} %slice_select_fusion.2), channel_id=1, source_target_pairs={{0,16},{1,9},{2,18},{3,11},{4,20},{5,13},{6,22},{7,15},{8,24},{9,1... | collective-permute-start | bytes 663560 | tf_op jit(solution)/shard_map/ppermute | solution.py:75
  304.9 6.3 %collective-permute-start.20 = (f32[27648]{0:T(1024)S(1)}, f32[27648]{0:T(1024)S(1)}, u32[]{:S(2)}, u32[]{:S(2)}) collective-permute-start(f32[27648]{0:T(1024)S(1)} %slice_select_fusion.3), channel_id=1, source_target_pairs={{0,4},{1,33},{2,6},{3,35},{4,0},{5,37},{6,2},{7,39},{8,12},{9,41},... | collective-permute-start | bytes 331784 | tf_op jit(solution)/shard_map/ppermute | solution.py:75
  311.3 5.8 %collective-permute-start.21 = (f32[13824]{0:T(1024)S(1)}, f32[13824]{0:T(1024)S(1)}, u32[]{:S(2)}, u32[]{:S(2)}) collective-permute-start(f32[13824]{0:T(1024)S(1)} %slice_select_fusion.4), channel_id=1, source_target_pairs={{0,128},{1,5},{2,130},{3,7},{4,132},{5,1},{6,134},{7,3},{8,136},{9... | collective-permute-start | bytes 165896 | tf_op jit(solution)/shard_map/ppermute | solution.py:75
  317.1 5.2 %collective-permute-start.22 = (f32[6912]{0:T(1024)S(1)}, f32[6912]{0:T(1024)S(1)}, u32[]{:S(2)}, u32[]{:S(2)}) collective-permute-start(f32[6912]{0:T(1024)S(1)} %slice_select_fusion.5), channel_id=1, source_target_pairs={{0,32},{1,129},{2,34},{3,131},{4,36},{5,133},{6,38},{7,135},{8,40}... | collective-permute-start | bytes 82952 | tf_op jit(solution)/shard_map/ppermute | solution.py:75
  322.3 7.7 %collective-permute-start.23 = (f32[3456]{0:T(1024)S(1)}, f32[3456]{0:T(1024)S(1)}, u32[]{:S(2)}, u32[]{:S(2)}) collective-permute-start(f32[3456]{0:T(1024)S(1)} %slice_select_fusion.6), channel_id=1, source_target_pairs={{0,64},{1,65},{2,66},{3,67},{4,68},{5,69},{6,70},{7,71},{8,72},{9,... | collective-permute-start | bytes 41480 | tf_op jit(solution)/shard_map/ppermute | solution.py:75
  330.0 7.6 %collective-permute-start.24 = (f32[3456]{0:T(1024)S(1)}, f32[3456]{0:T(1024)S(1)}, u32[]{:S(2)}, u32[]{:S(2)}) collective-permute-start(f32[3456]{0:T(1024)S(1)} %select_add_fusion.7), channel_id=1, source_target_pairs={{0,64},{1,65},{2,66},{3,67},{4,68},{5,69},{6,70},{7,71},{8,72},{9,... | collective-permute-start | bytes 41480 | tf_op jit(solution)/shard_map/ppermute | solution.py:78
  337.7 6.4 %collective-permute-start.25 = (f32[6912]{0:T(1024)S(1)}, f32[6912]{0:T(1024)S(1)}, u32[]{:S(2)}, u32[]{:S(2)}) collective-permute-start(f32[6912]{0:T(1024)S(1)} %maximum_select_fusion.13), channel_id=1, source_target_pairs={{0,32},{1,129},{2,34},{3,131},{4,36},{5,133},{6,38},{7,135},{8,40}... | collective-permute-start | bytes 82952 | tf_op jit(solution)/shard_map/ppermute | solution.py:78
  344.1 6.4 %collective-permute-start.26 = (f32[13824]{0:T(1024)S(1)}, f32[13824]{0:T(1024)S(1)}, u32[]{:S(2)}, u32[]{:S(2)}) collective-permute-start(f32[13824]{0:T(1024)S(1)} %maximum_select_fusion.10), channel_id=1, source_target_pairs={{0,128},{1,5},{2,130},{3,7},{4,132},{5,1},{6,134},{7,3},{8,136},{9... | collective-permute-start | bytes 165896 | tf_op jit(solution)/shard_map/ppermute | solution.py:78
  350.5 7.5 %collective-permute-start.27 = (f32[27648]{0:T(1024)S(1)}, f32[27648]{0:T(1024)S(1)}, u32[]{:S(2)}, u32[]{:S(2)}) collective-permute-start(f32[27648]{0:T(1024)S(1)} %maximum_select_fusion.8), channel_id=1, source_target_pairs={{0,4},{1,33},{2,6},{3,35},{4,0},{5,37},{6,2},{7,39},{8,12},{9,41},... | collective-permute-start | bytes 331784 | tf_op jit(solution)/shard_map/ppermute | solution.py:78
  358.1 8.4 %collective-permute-start.28 = (f32[55296]{0:T(1024)S(1)}, f32[55296]{0:T(1024)S(1)}, u32[]{:S(2)}, u32[]{:S(2)}) collective-permute-start(f32[55296]{0:T(1024)S(1)} %maximum_select_fusion.7), channel_id=1, source_target_pairs={{0,16},{1,9},{2,18},{3,11},{4,20},{5,13},{6,22},{7,15},{8,24},{9,1... | collective-permute-start | bytes 663560 | tf_op jit(solution)/shard_map/ppermute | solution.py:78
  366.5 23.8 %copy-start.36 = (f32[2,256]{1,0:T(2,128)S(1)}, f32[2,256]{1,0:T(2,128)}, u32[]{:S(2)}) copy-start(f32[2,256]{1,0:T(2,128)} %get-tuple-element.20) | copy-start | bytes 6148
  366.5 8.4 %collective-permute-start.29 = (f32[110592]{0:T(1024)S(1)}, f32[110592]{0:T(1024)S(1)}, u32[]{:S(2)}, u32[]{:S(2)}) collective-permute-start(f32[110592]{0:T(1024)S(1)} %maximum_select_fusion.5), channel_id=1, source_target_pairs={{0,8},{1,3},{2,10},{3,1},{4,12},{5,7},{6,14},{7,5},{8,0},{9,11},{1... | collective-permute-start | bytes 1327112 | tf_op jit(solution)/shard_map/ppermute | solution.py:78
  375.7 31.3 %copy-start.8 = (bf16[2,4,68,256]{3,1,2,0:T(4,128)(2,1)S(1)}, bf16[2,4,68,256]{3,1,2,0:T(4,128)(2,1)}, u32[]{:S(2)}) copy-start(bf16[2,4,68,256]{3,1,2,0:T(4,128)(2,1)} %param.11) | copy-start | bytes 835588
  375.7 31.3 %copy-start.38 = (f32[256]{0:T(256)S(1)}, f32[256]{0:T(256)}, u32[]{:S(2)}) copy-start(f32[256]{0:T(256)} %param.20) | copy-start | bytes 3076
  375.7 13.0 %collective-permute-start.30 = (f32[221184]{0:T(1024)S(1)}, f32[221184]{0:T(1024)S(1)}, u32[]{:S(2)}, u32[]{:S(2)}) collective-permute-start(f32[221184]{0:T(1024)S(1)} %maximum_select_fusion.3), channel_id=1, source_target_pairs={{0,2},{1,17},{2,0},{3,19},{4,6},{5,21},{6,4},{7,23},{8,10},{9,25},... | collective-permute-start | bytes 2654216 | tf_op jit(solution)/shard_map/ppermute | solution.py:78
  390.2 29.8 %collective-permute-start.31 = (f32[442368]{0:T(1024)}, f32[442368]{0:T(1024)S(1)}, u32[]{:S(2)}, u32[]{:S(2)}) collective-permute-start(f32[442368]{0:T(1024)} %maximum_select_fusion.1), channel_id=1, source_target_pairs={{0,1},{1,0},{2,3},{3,2},{4,5},{5,4},{6,7},{7,6},{8,9},{9,8},{10,11... | collective-permute-start | bytes 5308424 | tf_op jit(solution)/shard_map/ppermute | solution.py:78
  390.5 3.5 collective-permute-start.10
  394.1 3.6 collective-permute-start.11
  397.7 5.1 %collective-permute-start.12 = (f32[2,2,32]{2,1,0:T(2,128)S(1)}, f32[2,2,32]{2,1,0:T(2,128)S(1)}, u32[]{:S(2)}, u32[]{:S(2)}) collective-permute-start(f32[2,2,32]{2,1,0:T(2,128)S(1)} %fusion.153), channel_id=1, source_target_pairs={{0,4},{1,5},{2,6},{3,7},{4,0},{5,1},{6,2},{7,3},{8,12},{9,13},{10,... | collective-permute-start | bytes 1544 | tf_op jit(solution)/shard_map/ppermute | solution.py:34
  402.7 3.9 collective-permute-start.13
  419.9 3.0 copy-start.6
  426.5 3.5 copy-start.1
  (13 other events, 22.4 us)
Sparse Core Ops, SparseCore 0:
  10.4 40.2 all-gather.4
  52.6 40.3 all-gather.6
  95.4 40.4 all-gather.8
  138.1 40.0 all-gather.10
